TPU v7x, 256 devices: a whole 4x4x8 slice. The times are simulated.
256 devices in a mesh: gx: 8 (over y, core), gy: 8 (over z), ba: 4 (over x).
Axes of the slice: x: 4, y: 4, z: 8, core: 2. Of those that a mesh axis runs over, the one named last changes fastest.
Arguments:
- pixels: float32 [224, 128, 1024], P('ba', 'gy', 'gx'), may hold values from -8 to 8
- spectra: float32 [224, 256], P('ba'), may hold values from -0.375 to 0.375
- abundance: float32 [256, 128, 1024], P('ba', 'gy', 'gx'), may hold values from 0 to 1
- plan: int32 [3], replicated, may hold values from 0 to 1, as said below
Outputs:
- sparse: float32 [256, 128, 1024], P('ba', 'gy', 'gx')
- spectra_grad: float32 [224, 256], P('ba')
Inputs may be any that keep to these rules, and one draw needn't show every extreme that they name: `plan`: entry 0 is 1 and at least one later entry is 0.
All inputs are finite; a program needn't handle non-finite values. Where the computation divides by a largest or mean magnitude, that divisor is 1e-20 or more.
Results may differ from a plain program's by a relative error of at most 0.0001.
Values sent between devices are 32-bit elements; how exact they have to be, the bound alone decides.
No kernel may reach another device: no remote copies, remote signals or barrier semaphores. Data moves between devices by JAX's collectives and lax.ppermute only.
A program may use at most 64 MiB of HBM per device.

v0:
```python
import math
import jax
import jax.numpy as jnp
from jax import lax
from jax.sharding import PartitionSpec as P

SWEEPS = 3
HIGHEST = lax.Precision.HIGHEST
penalty = 1.0
tv_weight = 0.2
sparsity = 0.05


def extended_2(x, sides, width):
    for axis, dim in sides:
        size, length = (lax.axis_size(axis), x.shape[dim])
        up = [(i, (i + 1) % size) for i in range(size - 1)]
        down = [(j, i) for i, j in up]
        last = lax.slice_in_dim(x, length - width, length, axis=dim)
        leading = lax.slice_in_dim(x, 0, width, axis=dim)
        before = lax.ppermute(last, axis, up)
        after = lax.ppermute(leading, axis, down)
        x = jnp.concatenate([before, x, after], axis=dim)
    return x


def edge_masks(top_row, left_col, row_count, col_count, grid_rows, grid_cols):
    ext_rows = top_row - 1 + jnp.arange(row_count + 1)
    ext_cols = left_col - 1 + jnp.arange(col_count + 1)
    rows_in = (ext_rows >= 0) & (ext_rows <= grid_rows - 1)
    cols_in = (ext_cols >= 0) & (ext_cols <= grid_cols - 1)
    rows_ok = (ext_rows >= 0) & (ext_rows <= grid_rows - 2)
    cols_ok = (ext_cols >= 0) & (ext_cols <= grid_cols - 2)
    mask_h = (rows_in[:, None] & cols_ok[None, :]).astype(jnp.float32)[None]
    mask_v = (rows_ok[:, None] & cols_in[None, :]).astype(jnp.float32)[None]
    return (mask_h, mask_v)


def local(pixels, spectra, abundance, plan):
    comp_share, row_count, gx_cols = abundance.shape
    band_ways = lax.axis_size("ba")
    grid_rows = row_count * lax.axis_size("gy")
    grid_cols = gx_cols * lax.axis_size("gx")
    all_comps = comp_share * band_ways
    top_row = lax.axis_index("gy") * row_count
    all_spectra = lax.all_gather(spectra, "ba", axis=0, tiled=True)
    first_comp = lax.axis_index("ba") * comp_share
    own_cols = lax.dynamic_slice_in_dim(all_spectra, first_comp, comp_share, 1)
    gram_rows = jnp.dot(own_cols.T, all_spectra, precision=HIGHEST)
    bound = lax.pmax(jnp.max(jnp.sum(jnp.abs(gram_rows), axis=1)), "ba")
    left_col = lax.axis_index("gx") * gx_cols
    mask_h, mask_v = edge_masks(top_row, left_col, row_count, gx_cols, grid_rows, grid_cols)
    field = abundance
    sparse = abundance
    dual = jnp.zeros_like(abundance)
    weight = jnp.ones((comp_share, row_count + 1, gx_cols + 1), jnp.float32)
    for sweep in range(SWEEPS):
        extended = extended_2(field, (("gx", 2), ("gy", 1)), 1)
        center = extended[:, : row_count + 1, : gx_cols + 1]
        right = extended[:, : row_count + 1, 1:]
        below = extended[:, 1:, : gx_cols + 1]
        diff_h = (right - center) * mask_h
        diff_v = (below - center) * mask_v
        energy = diff_h * diff_h + diff_v * diff_v
        total = lax.psum(jnp.sum(energy[:, 1:, 1:]), ("gx", "gy", "ba"))
        smooth_sq = total / (all_comps * grid_rows * grid_cols) + 1e-06
        fresh = 1.0 / jnp.sqrt(energy + smooth_sq)
        weight = jnp.where(plan[sweep] == 1, fresh, weight)
        flux_h = weight * diff_h
        flux_v = weight * diff_v
        edge_h = weight * mask_h
        edge_v = weight * mask_v
        tv_grad = flux_h[:, 1:, :-1] - flux_h[:, 1:, 1:] + flux_v[:, :-1, 1:] - flux_v[:, 1:, 1:]
        degree = edge_h[:, 1:, 1:] + edge_h[:, 1:, :-1] + edge_v[:, 1:, 1:] + edge_v[:, :-1, 1:]
        mixed = jnp.einsum(
            "lq,qrc->lrc",
            spectra,
            lax.all_gather(field, "ba", axis=0, tiled=True),
            precision=HIGHEST,
        )
        resid = mixed - pixels
        data_grad = lax.psum_scatter(
            jnp.einsum("lp,lrc->prc", spectra, resid, precision=HIGHEST),
            "ba",
            scatter_dimension=0,
            tiled=True,
        )
        grad_total = data_grad + tv_weight * tv_grad + penalty * (field - sparse + dual)
        field = field - grad_total / (bound + penalty + 2.0 * tv_weight * degree)
        sparse = jnp.maximum(field + dual - sparsity / penalty, 0.0)
        dual = dual + field - sparse
    all_sparse = lax.all_gather(sparse, "ba", axis=0, tiled=True)
    resid = jnp.einsum("lp,prc->lrc", spectra, all_sparse, precision=HIGHEST) - pixels
    partial_grad = jnp.einsum("lrc,prc->lp", resid, all_sparse, precision=HIGHEST) / math.sqrt(
        grid_rows * grid_cols
    )
    spectra_grad = lax.psum(partial_grad, ("gx", "gy"))
    return (sparse, spectra_grad)


def solution(mesh):
    return jax.shard_map(
        local,
        mesh=mesh,
        in_specs=(P("ba", "gy", "gx"), P("ba", None), P("ba", "gy", "gx"), P()),
        out_specs=(P("ba", "gy", "gx"), P("ba", None)),
        check_vma=False,
    )
```

profile of v0, /device:TPU:2, one launch (start us, length us, event | category | flops | bytes accessed | tf_op | source)
XLA Modules:
  0.0 793.5 jit_solution(9205692723680209742)
XLA Ops:
  8.0 37.2 %all-gather.5.cloned.1.call-done = f32[256,16,128]{2,1,0:T(8,128)} async-done(((f32[64,16,128]{2,1,0:T(8,128)}), f32[256,16,128]{2,1,0:T(8,128)}) %all-gather.5.cloned.1.call-update) | async-done | bytes 2097168 | tf_op jit(solution)/shard_map/all_gather | solution.py:78
  45.1 3.5 fusion.4
  50.6 2.0 copy.19
  56.8 12.2 %all_gather.16 = f32[224,256]{1,0:T(8,128)S(1)} all-gather(f32[56,256]{1,0:T(8,128)S(1)} %copy-done.14), channel_id=1, replica_groups=mesh['gx'=8,'gy'=8,'ba'=4] {'ba'}, dimensions={0}, use_global_device_ids=true | all-gather | bytes 286720 | tf_op jit(solution)/shard_map/all_gather | solution.py:46
  70.8 3.5 collective-permute-start.2
  74.9 10.9 %pmax.7 = f32[]{:T(128)} all-reduce(f32[]{:T(128)} %reduce_max.9), channel_id=1, replica_groups=mesh['gx'=8,'gy'=8,'ba'=4] {'ba'}, use_global_device_ids=true, to_apply=%region_5.6 | all-reduce | flops 1 | bytes 8 | tf_op jit(solution)/shard_map/pmax | solution.py:50
  88.5 4.2 collective-permute-done.3
  96.1 78.7 %psum.28 = f32[]{:T(128)} all-reduce(f32[]{:T(128)} %slice_reduce_fusion.2), channel_id=1, replica_groups=mesh['gx'=8,'gy'=8,'ba'=4] {'gx','gy','ba'}, use_global_device_ids=true, to_apply=%region_2.0 | all-reduce | flops 1 | bytes 8 | tf_op jit(solution)/shard_map/psum | solution.py:65
  175.5 5.1 fusion.55
  180.6 6.1 fusion.45
  187.0 30.1 %all-gather.7.cloned.1.call-done = f32[256,16,128]{2,1,0:T(8,128)} async-done(((f32[64,16,128]{2,1,0:T(8,128)}), f32[256,16,128]{2,1,0:T(8,128)}) %all-gather.7.cloned.1.call-update) | async-done | bytes 2097168 | tf_op jit(solution)/shard_map/all_gather | solution.py:78
  217.1 3.5 fusion.2
  228.9 3.7 collective-permute-done.5
  233.1 3.5 collective-permute-start.6
  239.2 3.6 collective-permute-done.7
  246.3 83.2 %psum.29 = f32[]{:T(128)} all-reduce(f32[]{:T(128)} %slice_reduce_fusion.1), channel_id=1, replica_groups=mesh['gx'=8,'gy'=8,'ba'=4] {'gx','gy','ba'}, use_global_device_ids=true, to_apply=%region_8.9 | all-reduce | flops 1 | bytes 8 | tf_op jit(solution)/shard_map/psum | solution.py:65
  330.1 3.6 fusion.56
  334.9 2.7 fusion.68
  337.6 6.1 fusion.38
  344.0 29.8 %all-gather.9.cloned.1.call-done = f32[256,16,128]{2,1,0:T(8,128)} async-done(((f32[64,16,128]{2,1,0:T(8,128)}), f32[256,16,128]{2,1,0:T(8,128)}) %all-gather.9.cloned.1.call-update) | async-done | bytes 2097168 | tf_op jit(solution)/shard_map/all_gather | solution.py:78
  373.8 3.5 fusion
  385.6 3.7 collective-permute-done.9
  389.8 3.5 collective-permute-start.10
  395.9 3.6 collective-permute-done.11
  403.0 83.4 %psum.30 = f32[]{:T(128)} all-reduce(f32[]{:T(128)} %slice_reduce_fusion), channel_id=1, replica_groups=mesh['gx'=8,'gy'=8,'ba'=4] {'gx','gy','ba'}, use_global_device_ids=true, to_apply=%region_11.12 | all-reduce | flops 1 | bytes 8 | tf_op jit(solution)/shard_map/psum | solution.py:65
  487.1 3.7 fusion.57
  490.8 2.6 fusion.69
  493.4 6.1 fusion.49
  499.6 30.1 %all-gather.11.cloned.1.call-done = f32[256,16,128]{2,1,0:T(8,128)} async-done(((f32[64,16,128]{2,1,0:T(8,128)}), f32[256,16,128]{2,1,0:T(8,128)}) %all-gather.11.cloned.1.call-update) | async-done | bytes 2097168 | tf_op jit(solution)/shard_map/all_gather | solution.py:92
  529.7 3.7 fusion.6
  533.5 2.3 fusion.22
  535.8 250.9 %psum.31 = f32[56,256]{1,0:T(8,128)} all-reduce(f32[56,256]{1,0:T(8,128)S(1)} %fusion.22), channel_id=1, replica_groups=mesh['gx'=8,'gy'=8,'ba'=4] {'gx','gy'}, use_global_device_ids=true, to_apply=%region_12.13 | all-reduce | flops 14336 | bytes 114688 | tf_op jit(solution)/shard_map/psum | solution.py:97
  (96 shorter events, 44.2 us)
Async XLA Ops:
  7.2 41.5 %copy-start.10 = (f32[56,16,128]{2,1,0:T(8,128)S(1)}, f32[56,16,128]{2,1,0:T(8,128)}, u32[]{:S(2)}) copy-start(f32[56,16,128]{2,1,0:T(8,128)} %param.4) | copy-start | bytes 1376260
  7.2 38.0 %all-gather.5.cloned.1.call-start = ((), (), s32[]{:S(2)}) async-start(), calls=%async_computation.3 | async-start | bytes 2621440 | tf_op jit(solution)/shard_map/all_gather | solution.py:78
  7.9 40.9 %copy-start.14 = (f32[56,256]{1,0:T(8,128)S(1)}, f32[56,256]{1,0:T(8,128)}, u32[]{:S(2)}) copy-start(f32[56,256]{1,0:T(8,128)} %param.5) | copy-start | bytes 172036
  7.9 172.7 %reduce-scatter.4.cloned.1.call-start = ((), (), s32[]{:S(2)}) async-start(), calls=%async_computation.4 | async-start | bytes 2621440 | tf_op jit(solution)/shard_map/reduce_scatter | solution.py:82
  52.6 164.5 %all-gather.7.cloned.1.call-start = ((), (), s32[]{:S(2)}) async-start(), calls=%async_computation.5 | async-start | bytes 2621440 | tf_op jit(solution)/shard_map/all_gather | solution.py:78
  53.9 20.4 %copy-start.15 = (s32[3]{0:T(128)S(1)}, s32[3]{0:T(128)}, u32[]{:S(2)}) copy-start(s32[3]{0:T(128)} %param.7) | copy-start | bytes 40
  53.9 16.4 %collective-permute-start = (f32[64,16,1]{2,1,0:T(8,128)S(1)}, f32[64,16,1]{2,1,0:T(8,128)S(1)}, u32[]{:S(2)}, u32[]{:S(2)}) collective-permute-start(f32[64,16,1]{2,1,0:T(8,128)S(1)} %get-tuple-element.28), channel_id=1, source_target_pairs={{0,32},{32,64},{64,96},{96,128},{128,160},{160,192},{192,224},{1,3... | collective-permute-start | bytes 12296 | tf_op jit(solution)/shard_map/ppermute | solution.py:21
  55.5 14.8 %collective-permute-start.1 = (f32[64,16,1]{2,1,0:T(8,128)S(1)}, f32[64,16,1]{2,1,0:T(8,128)S(1)}, u32[]{:S(2)}, u32[]{:S(2)}) collective-permute-start(f32[64,16,1]{2,1,0:T(8,128)S(1)} %get-tuple-element.29), channel_id=1, source_target_pairs={{32,0},{64,32},{96,64},{128,96},{160,128},{192,160},{224,192},{33,... | collective-permute-start | bytes 12296 | tf_op jit(solution)/shard_map/ppermute | solution.py:22
  70.8 17.0 %collective-permute-start.2 = (f32[64,1,130]{2,1,0:T(1,128)S(1)}, f32[64,1,130]{2,1,0:T(1,128)S(1)}, u32[]{:S(2)}, u32[]{:S(2)}) collective-permute-start(f32[64,1,130]{2,1,0:T(1,128)S(1)} %get-tuple-element.23), channel_id=1, source_target_pairs={{0,4},{4,8},{8,12},{12,16},{16,20},{20,24},{24,28},{1,5},{5,9},{9,... | collective-permute-start | bytes 99848 | tf_op jit(solution)/shard_map/ppermute | solution.py:21
  86.5 6.2 collective-permute-start.3
  93.5 1.1 copy-start.3
  186.7 33.9 %copy-start.11 = (f32[56,16,128]{2,1,0:T(8,128)S(1)}, f32[56,16,128]{2,1,0:T(8,128)}, u32[]{:S(2)}) copy-start(f32[56,16,128]{2,1,0:T(8,128)} %param.4) | copy-start | bytes 1376260
  186.7 150.9 %reduce-scatter.6.cloned.1.call-start = ((), (), s32[]{:S(2)}) async-start(), calls=%async_computation.6 | async-start | bytes 2621440 | tf_op jit(solution)/shard_map/reduce_scatter | solution.py:82
  224.6 149.2 %all-gather.9.cloned.1.call-start = ((), (), s32[]{:S(2)}) async-start(), calls=%async_computation.7 | async-start | bytes 2621440 | tf_op jit(solution)/shard_map/all_gather | solution.py:78
  225.8 3.1 collective-permute-start.4
  227.4 5.2 collective-permute-start.5
  233.1 5.3 collective-permute-start.6
  236.6 6.2 collective-permute-start.7
  243.7 1.2 copy-start.6
  333.8 1.1 copy-start.4
  343.7 33.6 %copy-start.12 = (f32[56,16,128]{2,1,0:T(8,128)S(1)}, f32[56,16,128]{2,1,0:T(8,128)}, u32[]{:S(2)}) copy-start(f32[56,16,128]{2,1,0:T(8,128)} %param.4) | copy-start | bytes 1376260
  343.7 149.7 %reduce-scatter.8.cloned.1.call-start = ((), (), s32[]{:S(2)}) async-start(), calls=%async_computation.8 | async-start | bytes 2621440 | tf_op jit(solution)/shard_map/reduce_scatter | solution.py:82
  381.3 148.3 %all-gather.11.cloned.1.call-start = ((), (), s32[]{:S(2)}) async-start(), calls=%async_computation.9 | async-start | bytes 2621440 | tf_op jit(solution)/shard_map/all_gather | solution.py:92
  382.5 3.1 collective-permute-start.8
  384.1 5.2 collective-permute-start.9
  389.3 10.1 %copy-start.7 = (f32[64,16,1]{2,1,0:T(8,128)}, f32[64,16,1]{2,1,0:T(8,128)S(1)}, u32[]{:S(2)}) copy-start(f32[64,16,1]{2,1,0:T(8,128)S(1)} %collective-permute-done.9) | copy-start | bytes 12292
  389.8 5.3 collective-permute-start.10
  393.3 6.2 collective-permute-start.11
  400.4 1.2 copy-start.5
  487.1 3.7 copy-start.8
  499.6 33.8 %copy-start.13 = (f32[56,16,128]{2,1,0:T(8,128)S(1)}, f32[56,16,128]{2,1,0:T(8,128)}, u32[]{:S(2)}) copy-start(f32[56,16,128]{2,1,0:T(8,128)} %param.4) | copy-start | bytes 1376260
  529.6 3.8 copy-start.9
  (3 other events, 3.1 us)
Sparse Core Ops, SparseCore 0:
  9.8 35.2 all-gather.4
  52.8 32.7 reduce-scatter.3
  186.9 30.1 all-gather.6
  224.7 31.9 reduce-scatter.5
  343.9 29.8 all-gather.8
  381.4 31.9 reduce-scatter.7
  499.7 29.8 all-gather.10
where the time goes:
time: 795 us; the launch traced here: 794 us
  blocking collectives  519 us (65%)
  waiting for transfers between devices  148 us (19%)
  other arithmetic  46 us (6%)
  starting transfers between devices  23.6 us (3%)
  matrix products  22.7 us (3%)
  between operations  19.1 us (2%)
  local copies, waits for them, and re-layouts  14.7 us (2%)
    psum x1, blocking collectives, local(): spectra_grad = lax.psum(partial_grad, ('gx', 'gy'))  251 us
    psum x3, blocking collectives, local(): total = lax.psum(jnp.sum(energy[:, 1:, 1:]), ('gx', 'gy', 'ba'))  245 us
    all_gather x3, waiting for transfers between devices, local(): lax.all_gather(field, 'ba', axis=0, tiled=True)  97.1 us
    all_gather x1, waiting for transfers between devices, local(): all_sparse = lax.all_gather(sparse, 'ba', axis=0, tiled=True)  30.1 us
    ppermute x6, waiting for transfers between devices, extended_2(): after = lax.ppermute(leading, axis, down)  18.8 us
  transfers between devices with their start and end apart: 19, of which 13 were waited for; matrix products, arithmetic and copies ran while one was open for 4% of the time, Pallas kernels for 0%

commit v1 on v0

--- a/solution.py
+++ b/solution.py
@@ -9,6 +9,22 @@
 penalty = 1.0
 tv_weight = 0.2
 sparsity = 0.05
+
+
+def ring_product(x, axis, dim, term):
+    length, position, width = (lax.axis_size(axis), lax.axis_index(axis), x.shape[dim])
+    right = [(i, (i + 1) % length) for i in range(length)]
+    behind = [(i, (i - 1) % length) for i in range(length)]
+    halfway = length // 2
+    from_left = from_right = x
+    subtotal = term(x, position * width)
+    for lap in range(1, halfway + 1):
+        from_left = lax.ppermute(from_left, axis, right)
+        if lap < length - halfway:
+            from_right = lax.ppermute(from_right, axis, behind)
+            subtotal = subtotal + term(from_right, (position + lap) % length * width)
+        subtotal = subtotal + term(from_left, (position - lap) % length * width)
+    return subtotal
 
 
 def extended_2(x, sides, width):
@@ -72,11 +88,16 @@
         edge_v = weight * mask_v
         tv_grad = flux_h[:, 1:, :-1] - flux_h[:, 1:, 1:] + flux_v[:, :-1, 1:] - flux_v[:, 1:, 1:]
         degree = edge_h[:, 1:, 1:] + edge_h[:, 1:, :-1] + edge_v[:, 1:, 1:] + edge_v[:, :-1, 1:]
-        mixed = jnp.einsum(
-            "lq,qrc->lrc",
-            spectra,
-            lax.all_gather(field, "ba", axis=0, tiled=True),
-            precision=HIGHEST,
+        mixed = ring_product(
+            field,
+            "ba",
+            0,
+            lambda own_block, start: jnp.einsum(
+                "lq,qrc->lrc",
+                lax.dynamic_slice_in_dim(spectra, start, own_block.shape[0], axis=1),
+                own_block,
+                precision=HIGHEST,
+            ),
         )
         resid = mixed - pixels
         data_grad = lax.psum_scatter(

time: 795 us -> 776 us (0.976)
  waiting for transfers between devices: 148 us -> 112 us
    all_gather x3 -> x0, waiting for transfers between devices: 97.1 us -> none  [local(): lax.all_gather(field, 'ba', axis=0, tiled=True)]
    ppermute x0 -> x9, waiting for transfers between devices: none -> 63.3 us  [the longest x6 63.3 us: ring_product(): from_left = lax.ppermute(from_left, axis, right)]
    ppermute x0 -> x9, starting transfers between devices: none -> 10.9 us  [the longest x6 7.72 us: ring_product(): from_left = lax.ppermute(from_left, axis, right)]
  transfers between devices with their start and end apart: 19 -> 25, of which waited for: 13 -> 16; matrix products, arithmetic and copies ran while one was open for 4% -> 5% of each run, Pallas kernels for 0% -> 0%
where the time goes in v1:
time: 776 us; the launch traced here: 767 us
  blocking collectives  525 us (68%)
  waiting for transfers between devices  112 us (14%)
  other arithmetic  44.8 us (6%)
  starting transfers between devices  29.6 us (4%)
  matrix products  23.2 us (3%)
  between operations  19.3 us (2%)
  local copies, waits for them, and re-layouts  12.8 us (2%)
    psum x1, blocking collectives, local(): spectra_grad = lax.psum(partial_grad, ('gx', 'gy'))  251 us
    psum x3, blocking collectives, local(): total = lax.psum(jnp.sum(energy[:, 1:, 1:]), ('gx', 'gy', 'ba'))  250 us
    ppermute x6, waiting for transfers between devices, ring_product(): from_left = lax.ppermute(from_left, axis, right)  63.3 us
    all_gather x1, waiting for transfers between devices, local(): all_sparse = lax.all_gather(sparse, 'ba', axis=0, tiled=True)  30.1 us
    ppermute x6, waiting for transfers between devices, extended_2(): after = lax.ppermute(leading, axis, down)  17.2 us
  transfers between devices with their start and end apart: 25, of which 16 were waited for; matrix products, arithmetic and copies ran while one was open for 5% of the time, Pallas kernels for 0%

profile of v1, /device:TPU:2, one launch (start us, length us, event | category | flops | bytes accessed | tf_op | source)
XLA Modules:
  0.0 767.0 jit_solution(17329723712737660331)
XLA Ops:
  9.6 11.5 %collective-permute-done.1 = f32[64,16,128]{2,1,0:T(8,128)S(1)} collective-permute-done((f32[64,16,128]{2,1,0:T(8,128)}, f32[64,16,128]{2,1,0:T(8,128)S(1)}, u32[]{:S(2)}, u32[]{:S(2)}) %collective-permute-start.1) | collective-permute-done | bytes 524320 | tf_op jit(solution)/shard_map/ppermute | solution.py:22
  26.7 7.2 collective-permute-done.2
  37.7 2.0 copy.19
  43.6 13.4 %all_gather.6 = f32[224,256]{1,0:T(8,128)S(1)} all-gather(f32[56,256]{1,0:T(8,128)S(1)} %copy-done.12), channel_id=1, replica_groups=mesh['gx'=8,'gy'=8,'ba'=4] {'ba'}, dimensions={0}, use_global_device_ids=true | all-gather | bytes 286720 | tf_op jit(solution)/shard_map/all_gather | solution.py:62
  58.9 3.6 collective-permute-start.5
  63.1 11.3 %pmax.7 = f32[]{:T(128)} all-reduce(f32[]{:T(128)} %reduce_max.9), channel_id=1, replica_groups=mesh['gx'=8,'gy'=8,'ba'=4] {'ba'}, use_global_device_ids=true, to_apply=%region_5.6 | all-reduce | flops 1 | bytes 8 | tf_op jit(solution)/shard_map/pmax | solution.py:66
  77.1 4.2 collective-permute-done.6
  84.8 80.8 %psum.28 = f32[]{:T(128)} all-reduce(f32[]{:T(128)} %slice_reduce_fusion.2), channel_id=1, replica_groups=mesh['gx'=8,'gy'=8,'ba'=4] {'gx','gy','ba'}, use_global_device_ids=true, to_apply=%region_2.0 | all-reduce | flops 1 | bytes 8 | tf_op jit(solution)/shard_map/psum | solution.py:81
  166.2 5.1 fusion.76
  171.3 5.3 fusion.39
  178.8 11.7 %collective-permute-done.8 = f32[64,16,128]{2,1,0:T(8,128)S(1)} collective-permute-done((f32[64,16,128]{2,1,0:T(8,128)S(1)}, f32[64,16,128]{2,1,0:T(8,128)S(1)}, u32[]{:S(2)}, u32[]{:S(2)}) %collective-permute-start.8) | collective-permute-done | bytes 524320 | tf_op jit(solution)/shard_map/ppermute | solution.py:22
  193.2 10.8 %collective-permute-done.9 = f32[64,16,128]{2,1,0:T(8,128)S(1)} collective-permute-done((f32[64,16,128]{2,1,0:T(8,128)S(1)}, f32[64,16,128]{2,1,0:T(8,128)S(1)}, u32[]{:S(2)}, u32[]{:S(2)}) %collective-permute-start.9) | collective-permute-done | bytes 524320 | tf_op jit(solution)/shard_map/ppermute | solution.py:22
  206.8 2.0 copy.21
  211.9 3.3 collective-permute-done.11
  220.0 3.6 collective-permute-done.13
  227.2 83.9 %psum.29 = f32[]{:T(128)} all-reduce(f32[]{:T(128)} %slice_reduce_fusion.1), channel_id=1, replica_groups=mesh['gx'=8,'gy'=8,'ba'=4] {'gx','gy','ba'}, use_global_device_ids=true, to_apply=%region_8.9 | all-reduce | flops 1 | bytes 8 | tf_op jit(solution)/shard_map/psum | solution.py:81
  311.7 3.6 fusion.77
  316.4 2.7 fusion.122
  319.1 5.3 fusion.32
  327.3 11.6 %collective-permute-done.15 = f32[64,16,128]{2,1,0:T(8,128)S(1)} collective-permute-done((f32[64,16,128]{2,1,0:T(8,128)S(1)}, f32[64,16,128]{2,1,0:T(8,128)S(1)}, u32[]{:S(2)}, u32[]{:S(2)}) %collective-permute-start.15) | collective-permute-done | bytes 524320 | tf_op jit(solution)/shard_map/ppermute | solution.py:22
  342.4 10.5 %collective-permute-done.16 = f32[64,16,128]{2,1,0:T(8,128)S(1)} collective-permute-done((f32[64,16,128]{2,1,0:T(8,128)S(1)}, f32[64,16,128]{2,1,0:T(8,128)S(1)}, u32[]{:S(2)}, u32[]{:S(2)}) %collective-permute-start.16) | collective-permute-done | bytes 524320 | tf_op jit(solution)/shard_map/ppermute | solution.py:22
  355.8 2.0 copy.23
  360.8 2.5 collective-permute-done.18
  367.7 3.6 collective-permute-done.20
  374.8 85.1 %psum.30 = f32[]{:T(128)} all-reduce(f32[]{:T(128)} %slice_reduce_fusion), channel_id=1, replica_groups=mesh['gx'=8,'gy'=8,'ba'=4] {'gx','gy','ba'}, use_global_device_ids=true, to_apply=%region_11.12 | all-reduce | flops 1 | bytes 8 | tf_op jit(solution)/shard_map/psum | solution.py:81
  460.5 3.7 fusion.78
  464.2 2.6 fusion.123
  466.8 6.0 fusion.67
  472.8 30.1 %all-gather.2.cloned.1.call-done = f32[256,16,128]{2,1,0:T(8,128)} async-done(((f32[64,16,128]{2,1,0:T(8,128)}), f32[256,16,128]{2,1,0:T(8,128)}) %all-gather.2.cloned.1.call-update) | async-done | bytes 2097168 | tf_op jit(solution)/shard_map/all_gather | solution.py:113
  503.0 3.7 fusion
  506.8 2.3 fusion.16
  509.1 250.9 %psum.31 = f32[56,256]{1,0:T(8,128)} all-reduce(f32[56,256]{1,0:T(8,128)S(1)} %fusion.16), channel_id=1, replica_groups=mesh['gx'=8,'gy'=8,'ba'=4] {'gx','gy'}, use_global_device_ids=true, to_apply=%region_12.13 | all-reduce | flops 14336 | bytes 114688 | tf_op jit(solution)/shard_map/psum | solution.py:118
  (110 shorter events, 61.9 us)
Async XLA Ops:
  7.2 18.8 %copy-start.12 = (f32[56,256]{1,0:T(8,128)S(1)}, f32[56,256]{1,0:T(8,128)}, u32[]{:S(2)}) copy-start(f32[56,256]{1,0:T(8,128)} %param.5) | copy-start | bytes 172036
  7.2 164.2 %reduce-scatter.4.cloned.1.call-start = ((), (), s32[]{:S(2)}) async-start(), calls=%async_computation.3 | async-start | bytes 2621440 | tf_op jit(solution)/shard_map/reduce_scatter | solution.py:103
  7.2 14.0 %collective-permute-start.1 = (f32[64,16,128]{2,1,0:T(8,128)}, f32[64,16,128]{2,1,0:T(8,128)S(1)}, u32[]{:S(2)}, u32[]{:S(2)}) collective-permute-start(f32[64,16,128]{2,1,0:T(8,128)} %param.6), channel_id=1, source_target_pairs={{0,1},{1,2},{2,3},{3,0},{4,5},{5,6},{6,7},{7,4},{8,9},{9,10},{10,1... | collective-permute-start | bytes 1572872 | tf_op jit(solution)/shard_map/ppermute | solution.py:22
  8.8 17.2 %collective-permute-start = (f32[64,16,128]{2,1,0:T(8,128)}, f32[64,16,128]{2,1,0:T(8,128)S(1)}, u32[]{:S(2)}, u32[]{:S(2)}) collective-permute-start(f32[64,16,128]{2,1,0:T(8,128)} %param.6), channel_id=1, source_target_pairs={{0,3},{1,0},{2,1},{3,2},{4,7},{5,4},{6,5},{7,6},{8,11},{9,8},{10,9... | collective-permute-start | bytes 1572872 | tf_op jit(solution)/shard_map/ppermute | solution.py:24
  21.2 12.7 %collective-permute-start.2 = (f32[64,16,128]{2,1,0:T(8,128)S(1)}, f32[64,16,128]{2,1,0:T(8,128)}, u32[]{:S(2)}, u32[]{:S(2)}) collective-permute-start(f32[64,16,128]{2,1,0:T(8,128)S(1)} %collective-permute-done.1), channel_id=1, source_target_pairs={{0,1},{1,2},{2,3},{3,0},{4,5},{5,6},{6,7},{7,4},{8,9},{9,10},{10,1... | collective-permute-start | bytes 1572872 | tf_op jit(solution)/shard_map/ppermute | solution.py:22
  24.4 11.2 %copy-start.8 = (f32[56,16,128]{2,1,0:T(8,128)S(1)}, f32[56,16,128]{2,1,0:T(8,128)}, u32[]{:S(2)}) copy-start(f32[56,16,128]{2,1,0:T(8,128)} %param.4) | copy-start | bytes 1376260
  39.7 279.4 %reduce-scatter.6.cloned.1.call-start = ((), (), s32[]{:S(2)}) async-start(), calls=%async_computation.4 | async-start | bytes 2621440 | tf_op jit(solution)/shard_map/reduce_scatter | solution.py:103
  41.0 21.5 %copy-start.13 = (s32[3]{0:T(128)S(1)}, s32[3]{0:T(128)}, u32[]{:S(2)}) copy-start(s32[3]{0:T(128)} %param.7) | copy-start | bytes 40
  41.0 17.4 %collective-permute-start.3 = (f32[64,16,1]{2,1,0:T(8,128)S(1)}, f32[64,16,1]{2,1,0:T(8,128)S(1)}, u32[]{:S(2)}, u32[]{:S(2)}) collective-permute-start(f32[64,16,1]{2,1,0:T(8,128)S(1)} %get-tuple-element.28), channel_id=1, source_target_pairs={{0,32},{32,64},{64,96},{96,128},{128,160},{160,192},{192,224},{1,3... | collective-permute-start | bytes 12296 | tf_op jit(solution)/shard_map/ppermute | solution.py:37
  42.3 16.1 %collective-permute-start.4 = (f32[64,16,1]{2,1,0:T(8,128)S(1)}, f32[64,16,1]{2,1,0:T(8,128)S(1)}, u32[]{:S(2)}, u32[]{:S(2)}) collective-permute-start(f32[64,16,1]{2,1,0:T(8,128)S(1)} %get-tuple-element.29), channel_id=1, source_target_pairs={{32,0},{64,32},{96,64},{128,96},{160,128},{192,160},{224,192},{33,... | collective-permute-start | bytes 12296 | tf_op jit(solution)/shard_map/ppermute | solution.py:38
  58.9 17.5 %collective-permute-start.5 = (f32[64,1,130]{2,1,0:T(1,128)S(1)}, f32[64,1,130]{2,1,0:T(1,128)S(1)}, u32[]{:S(2)}, u32[]{:S(2)}) collective-permute-start(f32[64,1,130]{2,1,0:T(1,128)S(1)} %get-tuple-element.23), channel_id=1, source_target_pairs={{0,4},{4,8},{8,12},{12,16},{16,20},{20,24},{24,28},{1,5},{5,9},{9,... | collective-permute-start | bytes 99848 | tf_op jit(solution)/shard_map/ppermute | solution.py:37
  75.1 6.2 collective-permute-start.6
  176.7 13.8 %collective-permute-start.8 = (f32[64,16,128]{2,1,0:T(8,128)S(1)}, f32[64,16,128]{2,1,0:T(8,128)S(1)}, u32[]{:S(2)}, u32[]{:S(2)}) collective-permute-start(f32[64,16,128]{2,1,0:T(8,128)S(1)} %fusion.39), channel_id=1, source_target_pairs={{0,1},{1,2},{2,3},{3,0},{4,5},{5,6},{6,7},{7,4},{8,9},{9,10},{10,1... | collective-permute-start | bytes 1572872 | tf_op jit(solution)/shard_map/ppermute | solution.py:22
  177.4 15.1 %collective-permute-start.7 = (f32[64,16,128]{2,1,0:T(8,128)S(1)}, f32[64,16,128]{2,1,0:T(8,128)S(1)}, u32[]{:S(2)}, u32[]{:S(2)}) collective-permute-start(f32[64,16,128]{2,1,0:T(8,128)S(1)} %fusion.39), channel_id=1, source_target_pairs={{0,3},{1,0},{2,1},{3,2},{4,7},{5,4},{6,5},{7,6},{8,11},{9,8},{10,9... | collective-permute-start | bytes 1572872 | tf_op jit(solution)/shard_map/ppermute | solution.py:24
  190.4 13.6 %collective-permute-start.9 = (f32[64,16,128]{2,1,0:T(8,128)S(1)}, f32[64,16,128]{2,1,0:T(8,128)S(1)}, u32[]{:S(2)}, u32[]{:S(2)}) collective-permute-start(f32[64,16,128]{2,1,0:T(8,128)S(1)} %collective-permute-done.8), channel_id=1, source_target_pairs={{0,1},{1,2},{2,3},{3,0},{4,5},{5,6},{6,7},{7,4},{8,9},{9,10},{10,1... | collective-permute-start | bytes 1572872 | tf_op jit(solution)/shard_map/ppermute | solution.py:22
  191.8 12.9 %copy-start.9 = (f32[56,16,128]{2,1,0:T(8,128)S(1)}, f32[56,16,128]{2,1,0:T(8,128)}, u32[]{:S(2)}) copy-start(f32[56,16,128]{2,1,0:T(8,128)} %param.4) | copy-start | bytes 1376260
  208.8 258.0 %reduce-scatter.8.cloned.1.call-start = ((), (), s32[]{:S(2)}) async-start(), calls=%async_computation.5 | async-start | bytes 2621440 | tf_op jit(solution)/shard_map/reduce_scatter | solution.py:103
  209.1 2.8 collective-permute-start.10
  210.4 4.8 collective-permute-start.11
  215.7 3.6 collective-permute-start.12
  217.5 6.2 collective-permute-start.13
  324.5 14.4 %collective-permute-start.15 = (f32[64,16,128]{2,1,0:T(8,128)S(1)}, f32[64,16,128]{2,1,0:T(8,128)S(1)}, u32[]{:S(2)}, u32[]{:S(2)}) collective-permute-start(f32[64,16,128]{2,1,0:T(8,128)S(1)} %fusion.32), channel_id=1, source_target_pairs={{0,1},{1,2},{2,3},{3,0},{4,5},{5,6},{6,7},{7,4},{8,9},{9,10},{10,1... | collective-permute-start | bytes 1572872 | tf_op jit(solution)/shard_map/ppermute | solution.py:22
  326.4 15.3 %collective-permute-start.14 = (f32[64,16,128]{2,1,0:T(8,128)S(1)}, f32[64,16,128]{2,1,0:T(8,128)S(1)}, u32[]{:S(2)}, u32[]{:S(2)}) collective-permute-start(f32[64,16,128]{2,1,0:T(8,128)S(1)} %fusion.32), channel_id=1, source_target_pairs={{0,3},{1,0},{2,1},{3,2},{4,7},{5,4},{6,5},{7,6},{8,11},{9,8},{10,9... | collective-permute-start | bytes 1572872 | tf_op jit(solution)/shard_map/ppermute | solution.py:24
  338.9 14.0 %collective-permute-start.16 = (f32[64,16,128]{2,1,0:T(8,128)S(1)}, f32[64,16,128]{2,1,0:T(8,128)S(1)}, u32[]{:S(2)}, u32[]{:S(2)}) collective-permute-start(f32[64,16,128]{2,1,0:T(8,128)S(1)} %collective-permute-done.15), channel_id=1, source_target_pairs={{0,1},{1,2},{2,3},{3,0},{4,5},{5,6},{6,7},{7,4},{8,9},{9,10},{10,1... | collective-permute-start | bytes 1572872 | tf_op jit(solution)/shard_map/ppermute | solution.py:22
  341.0 12.6 %copy-start.10 = (f32[56,16,128]{2,1,0:T(8,128)S(1)}, f32[56,16,128]{2,1,0:T(8,128)}, u32[]{:S(2)}) copy-start(f32[56,16,128]{2,1,0:T(8,128)} %param.4) | copy-start | bytes 1376260
  357.8 145.2 %all-gather.2.cloned.1.call-start = ((), (), s32[]{:S(2)}) async-start(), calls=%async_computation.6 | async-start | bytes 2621440 | tf_op jit(solution)/shard_map/all_gather | solution.py:113
  358.0 2.8 collective-permute-start.17
  359.3 4.0 collective-permute-start.18
  363.3 8.0 %copy-start.5 = (f32[64,16,1]{2,1,0:T(8,128)}, f32[64,16,1]{2,1,0:T(8,128)S(1)}, u32[]{:S(2)}) copy-start(f32[64,16,1]{2,1,0:T(8,128)S(1)} %collective-permute-done.18) | copy-start | bytes 12292
  363.8 3.2 collective-permute-start.19
  365.1 6.2 collective-permute-start.20
  472.8 33.8 %copy-start.11 = (f32[56,16,128]{2,1,0:T(8,128)S(1)}, f32[56,16,128]{2,1,0:T(8,128)}, u32[]{:S(2)}) copy-start(f32[56,16,128]{2,1,0:T(8,128)} %param.4) | copy-start | bytes 1376260
  (7 other events, 13.2 us)
Sparse Core Ops, SparseCore 0:
  39.9 34.2 reduce-scatter.3
  209.0 29.0 reduce-scatter.5
  357.9 28.8 reduce-scatter.7
  473.0 29.9 all-gather.1
